TPU v7x, 512 devices: a whole 4x4x16 slice. The times are simulated.
512 devices in a mesh: dp: 4 (over x), ctx: 16 (over z), mp: 8 (over y, core).
Axes of the slice: x: 4, y: 4, z: 16, core: 2. Of those that a mesh axis runs over, the one named last changes fastest.
Arguments:
- tokens: bfloat16 [4, 2048, 4096], P('dp', 'ctx'), may hold values from -52 to 52
- x_weight: bfloat16 [4096, 8192], P(('dp', 'ctx'), 'mp'), may hold values from -0.09375 to 0.09375
- bc_weight: bfloat16 [4096, 1024], P(('dp', 'ctx'), 'mp'), may hold values from -0.09375 to 0.09375
- dt_weight: bfloat16 [4096, 128], P(('dp', 'ctx'), 'mp'), may hold values from -0.0234375 to 0.0234375
- conv_x: float32 [5, 8192], P(None, 'mp'), may hold values from -0.5 to 0.5
- conv_bc: float32 [5, 1024], P(None, 'mp'), may hold values from -0.5 to 0.5
- dt_bias: float32 [128], P('mp'), may hold values from -4.5 to -2.5
- a_log: float32 [128], P('mp')
- d_skip: float32 [128], P('mp'), may hold values from 0.5 to 1.5
- norm_gain: float32 [8192], P('mp'), may hold values from 0.5 to 1.5
Outputs:
- mixer_out: bfloat16 [4, 2048, 8192], P('dp', 'ctx', 'mp')
- kurtosis: float32 [4096], P('mp')
All inputs are finite; a program needn't handle non-finite values.
Results may differ from a plain program's by a relative error of at most 0.015.
Values may be sent and summed in bfloat16 or wider, within the bound.
No kernel may reach another device: no remote copies, remote signals or barrier semaphores. Data moves between devices by JAX's collectives and lax.ppermute only.
A program may use at most 64 MiB of HBM per device.

v0:
```python
import jax
import jax.numpy as jnp
from jax import lax
from jax.sharding import PartitionSpec as P

ROOT = 64
HEADS = 128
G = 4
NS = 128
HIGH = lax.Precision.HIGHEST


def passed_along(value, axis, steps):
    count = lax.axis_size(axis)
    first, last = (max(0, -steps), min(count, count - steps))
    return lax.ppermute(value, axis, [(source, source + steps) for source in range(first, last)])


def entering(decay, contrib, axis):
    length, place = (lax.axis_size(axis), lax.axis_index(axis))
    lanes = contrib.shape[-1]
    rows = contrib.size // lanes
    tail = jnp.zeros((8, lanes), jnp.float32).at[0, : decay.size].set(decay.reshape(-1))
    flat = jnp.concatenate([contrib.reshape(rows, lanes), tail]).astype(jnp.bfloat16)
    everything = lax.all_gather(flat, axis).astype(jnp.float32)
    states = everything[:, :rows].reshape((length,) + contrib.shape)
    decays = everything[:, rows, : decay.size].reshape((length,) + decay.shape)
    source = lax.broadcasted_iota(jnp.int32, (length, length), 0)
    between = lax.broadcasted_iota(jnp.int32, (length, length), 1)
    inside = jnp.logical_and(between > source, between < place)
    factors = jnp.where(inside[:, :, None, None], decays[None], 1.0)
    weights = jnp.prod(factors, 1)
    weights = jnp.where((source[:, 0] < place)[:, None, None], weights, 0.0)
    return jnp.einsum("jgh,jghpn->ghpn", weights, states, precision=HIGH)


def hadamard_signs(sign_order):
    row_index = lax.broadcasted_iota(jnp.int32, (sign_order, sign_order), 0)
    col_index = lax.broadcasted_iota(jnp.int32, (sign_order, sign_order), 1)
    common = jnp.bitwise_and(row_index, col_index)
    parity = jnp.zeros((sign_order, sign_order), jnp.int32)
    for bit_index in range(sign_order.bit_length() - 1):
        parity = parity + jnp.bitwise_and(jnp.right_shift(common, bit_index), 1)
    return 1.0 - 2.0 * jnp.bitwise_and(parity, 1).astype(jnp.float32)


def kurtosis_from(powers, row_count):
    average = powers[0] / row_count
    second = powers[1] / row_count - average * average
    fourth = (
        powers[3] / row_count
        - 4.0 * average * powers[2] / row_count
        + 6.0 * average * average * powers[1] / row_count
        - 3.0 * average * average * average * average
    )
    return fourth / (second * second + 1e-06)


def shards(
    tokens, x_weight, bc_weight, dt_weight, conv_x, conv_bc, dt_bias, a_log, d_skip, norm_gain
):
    tok_rows = tokens.shape[1]
    model_width = tokens.shape[2]
    signs = hadamard_signs(ROOT)
    blocks = tokens.reshape(tok_rows, ROOT, ROOT)
    first_pass = jnp.einsum(
        "tab,ac->tcb", blocks, signs.astype(jnp.bfloat16), preferred_element_type=jnp.float32
    )
    second = jnp.einsum("tcb,bd->tcd", first_pass, signs, precision=HIGH)
    rotated = (second.reshape(tok_rows, model_width) / ROOT).astype(jnp.bfloat16)
    channel_share = model_width // lax.axis_size("mp")
    own_cols = lax.dynamic_slice_in_dim(
        rotated, lax.axis_index("mp") * channel_share, channel_share, 1
    ).astype(jnp.float32)
    square = own_cols * own_cols
    powers = jnp.stack(
        [
            jnp.sum(own_cols, 0),
            jnp.sum(square, 0),
            jnp.sum(square * own_cols, 0),
            jnp.sum(square * square, 0),
        ]
    )
    row_count = float(tok_rows * lax.axis_size("dp") * lax.axis_size("ctx"))
    totals = lax.psum(lax.psum(powers, "ctx"), "dp")
    totals, rotated = lax.optimization_barrier((totals, rotated))
    kurtosis = kurtosis_from(totals, row_count)
    local_panel = jnp.concatenate([x_weight, bc_weight, dt_weight], 1)
    panel = lax.all_gather(local_panel, ("dp", "ctx"), axis=0, tiled=True)
    both = jnp.dot(rotated, panel, preferred_element_type=jnp.float32)
    x_end = x_weight.shape[1]
    bc_end = x_end + bc_weight.shape[1]
    projected = (both[:, :x_end], both[:, x_end:bc_end], both[:, bc_end:])
    x_cols = x_weight.shape[1]
    joined = jnp.concatenate(
        [projected[0].astype(jnp.bfloat16), projected[1].astype(jnp.bfloat16)], 1
    )
    dt_proj = lax.optimization_barrier(projected[2].astype(jnp.bfloat16))
    conv_taps = jnp.concatenate([conv_x, conv_bc], 1)
    kernel = conv_taps.shape[0] - 1
    rim_rows = passed_along(joined[tok_rows - (kernel - 1) :], "ctx", 1)
    padded = jnp.concatenate([rim_rows, joined], 0)
    conv_sum = conv_taps[kernel]
    for tap_index in range(kernel):
        conv_sum = conv_sum + conv_taps[tap_index] * padded[tap_index : tap_index + tok_rows]
    convolved = jax.nn.silu(conv_sum).astype(jnp.bfloat16)
    x_conv = convolved[:, :x_cols]
    group_all = lax.all_gather(convolved[:, x_cols:], "mp", axis=1, tiled=True)
    heads_dev = dt_weight.shape[1]
    head_size = x_cols // heads_dev
    per_group = HEADS // G
    groups_here = max(1, heads_dev // per_group)
    heads_local = heads_dev // groups_here
    first_group = lax.axis_index("mp") * heads_dev // per_group
    write_all = group_all[:, : G * NS].reshape(tok_rows, G, NS)
    read_all = group_all[:, G * NS :].reshape(tok_rows, G, NS)
    write_here = lax.dynamic_slice_in_dim(write_all, first_group, groups_here, 1)
    read_here = lax.dynamic_slice_in_dim(read_all, first_group, groups_here, 1)
    step_size = jax.nn.softplus(dt_proj.astype(jnp.float32) + dt_bias)
    decay_rate = step_size * jnp.exp(a_log)
    cumulative = jnp.cumsum(decay_rate, 0)
    block_end = cumulative[-1]
    causal = lax.broadcasted_iota(jnp.int32, (tok_rows, tok_rows), 0) >= lax.broadcasted_iota(
        jnp.int32, (tok_rows, tok_rows), 1
    )
    spread = cumulative.T[:, :, None] - cumulative.T[:, None, :]
    decay_mask = jnp.where(causal, jnp.exp(-jnp.where(causal, spread, 0.0)), 0.0)
    scores = jnp.einsum("tgn,sgn->gts", read_here, write_here, preferred_element_type=jnp.float32)
    weights = (
        scores[:, None]
        * decay_mask.reshape(groups_here, heads_local, tok_rows, tok_rows)
        * step_size.T.reshape(groups_here, heads_local, 1, tok_rows)
    ).astype(jnp.bfloat16)
    x_heads = x_conv.reshape(tok_rows, groups_here, heads_local, head_size)
    within_block = jnp.einsum(
        "ghts,sghp->tghp", weights, x_heads, preferred_element_type=jnp.float32
    )
    update = (
        (jnp.exp(-(block_end - cumulative)) * step_size).reshape(
            tok_rows, groups_here, heads_local
        )[..., None]
        * x_heads
    ).astype(jnp.bfloat16)
    contrib = jnp.einsum("sghp,sgn->ghpn", update, write_here, preferred_element_type=jnp.float32)
    carried = entering(jnp.exp(-block_end).reshape(groups_here, heads_local), contrib, "ctx")
    from_before = jnp.exp(-cumulative).reshape(tok_rows, groups_here, heads_local)[
        ..., None
    ] * jnp.einsum("tgn,ghpn->tghp", read_here.astype(jnp.float32), carried, precision=HIGH)
    output_raw = (
        within_block
        + from_before
        + d_skip.reshape(groups_here, heads_local)[None, :, :, None] * x_heads.astype(jnp.float32)
    )
    mean_square = jnp.mean(output_raw * output_raw, -1, keepdims=True)
    normed = (
        output_raw
        * lax.rsqrt(mean_square + 1e-05)
        * norm_gain.reshape(groups_here, heads_local, head_size)
    )
    return (normed.reshape(1, tok_rows, x_cols).astype(jnp.bfloat16), kurtosis)


def solution(mesh):
    return jax.shard_map(
        shards,
        mesh=mesh,
        in_specs=(
            P("dp", "ctx", None),
            P(("dp", "ctx"), "mp"),
            P(("dp", "ctx"), "mp"),
            P(("dp", "ctx"), "mp"),
            P(None, "mp"),
            P(None, "mp"),
            P("mp"),
            P("mp"),
            P("mp"),
            P("mp"),
        ),
        out_specs=(P("dp", "ctx", "mp"), P("mp")),
        check_vma=False,
    )
```

profile of v0, /device:TPU:4, one launch (start us, length us, event | category | flops | bytes accessed | tf_op | source)
XLA Modules:
  0.0 302.1 jit_solution(1857820000837005802)
XLA Ops:
  7.2 0.0 all-gather.3.cloned.1.call-start
  7.2 0.8 copy.43
  8.0 1.6 pad_maximum_fusion.1
  9.6 0.0 all-gather.3.cloned.1.call-update
  9.6 0.0 all-gather.5.cloned.1.call-start
  9.7 0.0 copy-start.5
  9.7 0.0 copy-start.1
  9.7 0.0 copy-start.3
  9.7 1.6 copy.40
  11.3 0.9 convolution_bitcast_fusion
  12.2 3.3 %multiply_convert_fusion = bf16[128,64,64]{0,2,1:T(8,128)(2,1)S(1)} fusion(f32[128,64,64]{0,1,2:T(8,128)S(1)} %convolution_bitcast_fusion), kind=kOutput, calls=%fused_computation.5 | convolution fusion | flops 403791872 | bytes 3145728 | tf_op jit(solution)/shard_map/tcb,bd->tcd/dot_general | solution.py:69
  15.6 0.3 convert_reduce_fusion
  15.9 37.2 %psum.14 = f32[4,512]{1,0:T(4,128)S(1)} all-reduce(f32[4,512]{1,0:T(4,128)S(1)} %pad_maximum_fusion.2), channel_id=1, replica_groups=mesh['dp'=4,'ctx'=16,'mp'=8] {'ctx'}, use_global_device_ids=true, to_apply=%region_4.0 | all-reduce | flops 2048 | bytes 16384 | tf_op jit(solution)/shard_map/psum | solution.py:85
  53.1 8.4 %psum.15 = f32[4,512]{1,0:T(4,128)S(1)} all-reduce(f32[4,512]{1,0:T(4,128)S(1)} %psum.14), channel_id=1, replica_groups=mesh['dp'=4,'ctx'=16,'mp'=8] {'dp'}, use_global_device_ids=true, to_apply=%region_5.0 | all-reduce | flops 2048 | bytes 16384 | tf_op jit(solution)/shard_map/psum | solution.py:85
  61.6 0.1 slice_reduce_fusion.4
  61.7 0.0 copy-start.4
  61.7 116.0 %all-gather.3.cloned.1.call-done = bf16[4096,1168]{1,0:T(8,128)(2,1)} async-done(((bf16[64,1168]{1,0:T(8,128)(2,1)}), bf16[4096,1168]{1,0:T(8,128)(2,1)}) %all-gather.3.cloned.1.call-update) | async-done | bytes 9568272 | tf_op jit(solution)/shard_map/all_gather | solution.py:89
  177.7 8.0 %convolution_convert_fusion = bf16[128,1168]{0,1:T(8,128)(2,1)S(1)} fusion(bf16[128,4096]{0,1:T(8,128)(2,1)S(1)} %bitcast.81, bf16[4096,1168]{1,0:T(8,128)(2,1)} %all-gather.3.cloned.1.call-done), kind=kOutput, calls=%fused_computation.2 | convolution fusion | flops 1224886272 | bytes 10915840 | tf_op jit(solution)/shard_map/dot_general | solution.py:90
  185.7 0.1 slice.121
  185.9 0.1 broadcast_multiply_fusion
  186.0 0.1 copy.45
  186.1 0.2 reduce_window_sum.11
  186.2 0.1 copy.49
  186.3 3.3 %collective-permute-start = (bf16[3,1152]{0,1:T(8,128)(2,1)S(1)}, bf16[3,1152]{0,1:T(8,128)(2,1)S(1)}, u32[]{:S(2)}, u32[]{:S(2)}) collective-permute-start(bf16[3,1152]{0,1:T(8,128)(2,1)S(1)} %slice.121), channel_id=1, source_target_pairs={{0,8},{8,16},{16,24},{24,32},{32,40},{40,48},{48,56},{56,64},{64,7... | collective-permute-start | bytes 20744 | tf_op jit(solution)/shard_map/ppermute | solution.py:16
  189.6 0.1 fusion.60
  189.7 4.1 %collective-permute-done = bf16[3,1152]{0,1:T(8,128)(2,1)S(1)} collective-permute-done((bf16[3,1152]{0,1:T(8,128)(2,1)S(1)}, bf16[3,1152]{0,1:T(8,128)(2,1)S(1)}, u32[]{:S(2)}, u32[]{:S(2)}) %collective-permute-start) | collective-permute-done | bytes 6944 | tf_op jit(solution)/shard_map/ppermute | solution.py:16
  193.8 1.4 multiply_convert_fusion.2
  195.2 13.4 %all_gather.11 = bf16[128,1024]{0,1:T(8,128)(2,1)S(1)} all-gather(bf16[128,128]{0,1:T(8,128)(2,1)S(1)} %slice.131), channel_id=1, replica_groups=mesh['dp'=4,'ctx'=16,'mp'=8] {'mp'}, dimensions={1}, use_global_device_ids=true | all-gather | bytes 294912 | tf_op jit(solution)/shard_map/all_gather | solution.py:108
  208.6 0.1 multiply_convert_fusion.5
  208.7 0.2 fusion.9
  208.9 0.7 fusion.22
  209.7 0.0 all-gather.5.cloned.1.call-update
  209.7 0.1 mul.242
  209.8 0.6 fusion.39
  210.5 0.1 copy.48
  210.5 0.1 copy.46
  210.6 0.2 fusion.26
  210.8 75.6 %all-gather.5.cloned.1.call-done = bf16[16,1032,128]{2,1,0:T(8,128)(2,1)} async-done(((bf16[1,1032,128]{2,1,0:T(8,128)(2,1)}), bf16[16,1032,128]{2,1,0:T(8,128)(2,1)}) %all-gather.5.cloned.1.call-update) | async-done | bytes 4227088 | tf_op jit(solution)/shard_map/all_gather | solution.py:25
  286.3 0.8 slice_convert_fusion
  287.1 0.1 select_reduce_fusion
  287.2 0.1 select_bitcast_fusion
  287.3 0.1 copy.51
  287.4 2.2 slice-done
  289.6 3.6 %fusion = f32[16,1,64,128]{3,1,2,0:T(1,128)S(1)} fusion(f32[16,16,1,1]{0,2,3,1:T(1,128)S(1)} %copy.51, bf16[16,16,64,128]{3,2,1,0:T(8,128)(2,1)S(1)} %bitcast.79), kind=kOutput, calls=%fused_computation | convolution fusion | flops 25165824 | bytes 4719616 | tf_op jit(solution)/shard_map/jgh,jghpn->ghpn/dot_general | solution.py:34
  293.1 0.4 fusion.8
  293.5 0.6 multiply_reduce_fusion
  294.2 0.2 multiply_convert_fusion.4
  294.4 0.9 copy.50
  (29 shorter events, 0.2 us)
Async XLA Ops:
  7.2 170.5 %all-gather.3.cloned.1.call-start = ((), (), s32[]{:S(2)}) async-start(), calls=%async_computation | async-start | bytes 10649600 | tf_op jit(solution)/shard_map/all_gather | solution.py:89
  9.6 276.7 %all-gather.5.cloned.1.call-start = ((), (), s32[]{:S(2)}) async-start(), calls=%async_computation.1 | async-start | bytes 4491264 | tf_op jit(solution)/shard_map/all_gather | solution.py:25
  9.7 51.8 %copy-start.5 = (f32[16]{0:T(128)S(1)}, f32[16]{0:T(128)}, u32[]{:S(2)}) copy-start(f32[16]{0:T(128)} %param.19) | copy-start | bytes 196
  9.7 51.9 %copy-start.1 = (f32[5,1024]{1,0:T(8,128)S(1)}, f32[5,1024]{1,0:T(8,128)}, u32[]{:S(2)}) copy-start(f32[5,1024]{1,0:T(8,128)} %param.16) | copy-start | bytes 61444
  9.7 51.9 %copy-start.3 = (f32[5,128]{1,0:T(8,128)S(1)}, f32[5,128]{1,0:T(8,128)}, u32[]{:S(2)}) copy-start(f32[5,128]{1,0:T(8,128)} %param.17) | copy-start | bytes 7684
  61.7 124.2 %copy-start.4 = (f32[16]{0:T(128)S(1)}, f32[16]{0:T(128)}, u32[]{:S(2)}) copy-start(f32[16]{0:T(128)} %param.18) | copy-start | bytes 196
  185.7 24.0 %copy-start.2 = (f32[1024]{0:T(1024)S(1)}, f32[1024]{0:T(1024)}, u32[]{:S(2)}) copy-start(f32[1024]{0:T(1024)} %param.21) | copy-start | bytes 12292
  186.3 7.5 %collective-permute-start = (bf16[3,1152]{0,1:T(8,128)(2,1)S(1)}, bf16[3,1152]{0,1:T(8,128)(2,1)S(1)}, u32[]{:S(2)}, u32[]{:S(2)}) collective-permute-start(bf16[3,1152]{0,1:T(8,128)(2,1)S(1)} %slice.121), channel_id=1, source_target_pairs={{0,8},{8,16},{16,24},{24,32},{32,40},{40,48},{48,56},{56,64},{64,7... | collective-permute-start | bytes 20744 | tf_op jit(solution)/shard_map/ppermute | solution.py:16
  195.2 92.2 %copy-start = (bf16[128,1152]{0,1:T(8,128)(2,1)}, bf16[128,1152]{0,1:T(8,128)(2,1)S(1)}, u32[]{:S(2)}) copy-start(bf16[128,1152]{0,1:T(8,128)(2,1)S(1)} %multiply_convert_fusion.2) | copy-start | bytes 884740
  287.4 2.2 slice-start
  287.4 6.1 %copy-start.6 = (f32[16]{0:T(128)S(1)}, f32[16]{0:T(128)}, u32[]{:S(2)}) copy-start(f32[16]{0:T(128)} %param.20) | copy-start | bytes 196
  289.6 4.0 %slice-start.1 = ((bf16[128,1152]{0,1:T(8,128)(2,1)}), bf16[128,1024]{0,1:T(8,128)(2,1)S(1)}, s32[]{:S(2)}) async-start(bf16[128,1152]{0,1:T(8,128)(2,1)} %copy-done), calls=%async_computation.3 | async-start | bytes 524288 | tf_op jit(solution)/shard_map/slice | solution.py:107
Sparse Core Ops, SparseCore 0:
  11.5 166.0 all-gather.2
  209.8 76.4 all-gather.4
where the time goes:
time: 302 us
  waiting for transfers between devices  196 us (65%)
  blocking collectives  58.9 us (20%)
  matrix products  17.2 us (6%)
  between operations  14.4 us (5%)
  other arithmetic  6.37 us (2%)
  local copies, waits for them, and re-layouts  6.17 us (2%)
  starting transfers between devices  3.33 us (1%)
    all_gather x1, waiting for transfers between devices, shards(): panel = lax.all_gather(local_panel, ('dp', 'ctx'), axis=0, tiled=True)  116 us
    all_gather x1, waiting for transfers between devices, entering(): everything = lax.all_gather(flat, axis).astype(jnp.float32)  75.6 us
    psum x2, blocking collectives, shards(): totals = lax.psum(lax.psum(powers, 'ctx'), 'dp')  45.6 us
    all_gather x1, blocking collectives, shards(): group_all = lax.all_gather(convolved[:, x_cols:], 'mp', axis=1, tiled=True)  13.4 us
    dot_general x1, matrix products, shards(): both = jnp.dot(rotated, panel, preferred_element_type=jnp.float32)  8.01 us
  transfers between devices with their start and end apart: 3, of which 3 were waited for; matrix products, arithmetic and copies ran while one was open for 2% of the time, Pallas kernels for 0%

commit v1 on v0

--- a/solution.py
+++ b/solution.py
@@ -8,6 +8,13 @@
 G = 4
 NS = 128
 HIGH = lax.Precision.HIGHEST
+
+
+def fill_the_tracks(shard_in):
+    s_next = jnp.stack([shard_in for _ in range(jax.lax.axis_size(("dp", "ctx")))], 0)
+    local_part = jax.lax.all_to_all(s_next, ("dp", "ctx"), 0, 0)
+    after = jnp.concatenate(local_part, 0)
+    return after
 
 
 def passed_along(value, axis, steps):
@@ -86,7 +93,7 @@
     totals, rotated = lax.optimization_barrier((totals, rotated))
     kurtosis = kurtosis_from(totals, row_count)
     local_panel = jnp.concatenate([x_weight, bc_weight, dt_weight], 1)
-    panel = lax.all_gather(local_panel, ("dp", "ctx"), axis=0, tiled=True)
+    panel = fill_the_tracks(local_panel)
     both = jnp.dot(rotated, panel, preferred_element_type=jnp.float32)
     x_end = x_weight.shape[1]
     bc_end = x_end + bc_weight.shape[1]

time: 302 us -> 644 us (2.13)
  the two profiles are of different devices: /device:TPU:4 before, /device:TPU:2 now
where the time goes in v1:
time: 644 us
  blocking collectives  492 us (76%)
  waiting for transfers between devices  83.2 us (13%)
  starting transfers between devices  20.7 us (3%)
  matrix products  17.2 us (3%)
  between operations  14.4 us (2%)
  local copies, waits for them, and re-layouts  10.3 us (2%)
    psum x2, blocking collectives, shards(): totals = lax.psum(lax.psum(powers, 'ctx'), 'dp')  479 us
    all_gather x1, waiting for transfers between devices, entering(): everything = lax.all_gather(flat, axis).astype(jnp.float32)  79.2 us
    all_to_all x1, starting transfers between devices, fill_the_tracks(): local_part = jax.lax.all_to_all(s_next, ('dp', 'ctx'), 0, 0)  18.9 us
    all_gather x1, blocking collectives, shards(): group_all = lax.all_gather(convolved[:, x_cols:], 'mp', axis=1, tiled=True)  13.4 us
  transfers between devices with their start and end apart: 3, of which 2 were waited for; matrix products, arithmetic and copies ran while one was open for 1% of the time, Pallas kernels for 0%

profile of v1, /device:TPU:2, one launch (start us, length us, event | category | flops | bytes accessed | tf_op | source)
XLA Modules:
  0.0 643.8 jit_solution(1447151864061325425)
XLA Ops:
  7.2 0.8 copy.43
  7.9 0.9 pad_maximum_fusion.1
  8.9 5.1 stack.17
  14.0 18.9 %all-to-all-start = ((bf16[64,64,1168]{2,1,0:T(8,128)(2,1)}), bf16[64,64,1168]{2,1,0:T(8,128)(2,1)}, u32[]{:S(2)}, u32[]{:S(2)}) async-start(bf16[64,64,1168]{2,1,0:T(8,128)(2,1)} %stack.17), calls=%async_computation | async-start | bytes 20971520 | tf_op jit(solution)/shard_map/all_to_all | solution.py:15
  32.9 0.0 all-gather.2.cloned.1.call-start
  33.0 0.0 copy-start.6
  33.0 0.0 copy-start.2
  33.0 0.0 copy-start.4
  33.1 0.7 copy.40
  33.7 0.9 convolution_bitcast_fusion
  34.6 3.3 multiply_convert_fusion
  37.9 0.3 convert_reduce_fusion
  38.3 469.9 %psum.14 = f32[4,512]{1,0:T(4,128)S(1)} all-reduce(f32[4,512]{1,0:T(4,128)S(1)} %pad_maximum_fusion.2), channel_id=1, replica_groups=mesh['dp'=4,'ctx'=16,'mp'=8] {'ctx'}, use_global_device_ids=true, to_apply=%region_4.0 | all-reduce | flops 2048 | bytes 16384 | tf_op jit(solution)/shard_map/psum | solution.py:92
  508.2 9.0 %psum.15 = f32[4,512]{1,0:T(4,128)S(1)} all-reduce(f32[4,512]{1,0:T(4,128)S(1)} %psum.14), channel_id=1, replica_groups=mesh['dp'=4,'ctx'=16,'mp'=8] {'dp'}, use_global_device_ids=true, to_apply=%region_5.0 | all-reduce | flops 2048 | bytes 16384 | tf_op jit(solution)/shard_map/psum | solution.py:92
  517.3 0.1 slice_reduce_fusion.4
  517.4 0.0 copy-start.5
  517.4 8.0 %convolution_convert_fusion = bf16[128,1168]{0,1:T(8,128)(2,1)S(1)} fusion(bf16[128,4096]{0,1:T(8,128)(2,1)S(1)} %bitcast.82, bf16[4096,1168]{1,0:T(8,128)(2,1)} %bitcast.9), kind=kOutput, calls=%fused_computation.2 | convolution fusion | flops 1224886272 | bytes 10915840 | tf_op jit(solution)/shard_map/dot_general | solution.py:97
  525.4 0.0 copy-start.3
  525.5 0.1 slice.121
  525.6 0.1 broadcast_multiply_fusion
  525.7 0.1 copy.45
  525.8 0.2 reduce_window_sum.11
  526.0 0.1 copy.49
  526.1 1.7 collective-permute-start
  527.8 0.1 fusion.60
  527.9 3.9 collective-permute-done
  531.8 1.4 multiply_convert_fusion.2
  533.3 13.4 %all_gather.7 = bf16[128,1024]{0,1:T(8,128)(2,1)S(1)} all-gather(bf16[128,128]{0,1:T(8,128)(2,1)S(1)} %slice.131), channel_id=1, replica_groups=mesh['dp'=4,'ctx'=16,'mp'=8] {'mp'}, dimensions={1}, use_global_device_ids=true | all-gather | bytes 294912 | tf_op jit(solution)/shard_map/all_gather | solution.py:115
  546.7 0.1 multiply_convert_fusion.5
  546.7 0.2 fusion.9
  547.0 0.7 fusion.22
  547.7 0.0 all-gather.2.cloned.1.call-update
  547.7 0.1 mul.242
  547.9 0.6 fusion.39
  548.5 0.1 copy.48
  548.6 0.1 copy.46
  548.6 0.2 fusion.26
  548.8 79.2 %all-gather.2.cloned.1.call-done = bf16[16,1032,128]{2,1,0:T(8,128)(2,1)} async-done(((bf16[1,1032,128]{2,1,0:T(8,128)(2,1)}), bf16[16,1032,128]{2,1,0:T(8,128)(2,1)}) %all-gather.2.cloned.1.call-update) | async-done | bytes 4227088 | tf_op jit(solution)/shard_map/all_gather | solution.py:32
  628.1 0.8 slice_convert_fusion
  628.8 0.1 select_reduce_fusion
  629.0 0.1 select_bitcast_fusion
  629.0 0.1 copy.51
  629.1 2.2 slice-done
  631.3 3.6 fusion
  634.9 0.4 fusion.8
  635.3 0.6 multiply_reduce_fusion
  635.9 0.2 multiply_convert_fusion.4
  636.1 0.9 copy.50
  (31 shorter events, 0.2 us)
Async XLA Ops:
  14.0 19.0 %copy-start.1 = (bf16[1,128,4096]{2,1,0:T(8,128)(2,1)S(1)}, bf16[1,128,4096]{2,1,0:T(8,128)(2,1)}, u32[]{:S(2)}) copy-start(bf16[1,128,4096]{2,1,0:T(8,128)(2,1)} %param.12) | copy-start | bytes 3145732
  14.0 503.4 %all-to-all-start = ((bf16[64,64,1168]{2,1,0:T(8,128)(2,1)}), bf16[64,64,1168]{2,1,0:T(8,128)(2,1)}, u32[]{:S(2)}, u32[]{:S(2)}) async-start(bf16[64,64,1168]{2,1,0:T(8,128)(2,1)} %stack.17), calls=%async_computation | async-start | bytes 20971520 | tf_op jit(solution)/shard_map/all_to_all | solution.py:15
  32.9 595.1 %all-gather.2.cloned.1.call-start = ((), (), s32[]{:S(2)}) async-start(), calls=%async_computation.1 | async-start | bytes 4491264 | tf_op jit(solution)/shard_map/all_gather | solution.py:32
  33.0 484.2 %copy-start.6 = (f32[16]{0:T(128)S(1)}, f32[16]{0:T(128)}, u32[]{:S(2)}) copy-start(f32[16]{0:T(128)} %param.19) | copy-start | bytes 196
  33.0 484.3 %copy-start.2 = (f32[5,1024]{1,0:T(8,128)S(1)}, f32[5,1024]{1,0:T(8,128)}, u32[]{:S(2)}) copy-start(f32[5,1024]{1,0:T(8,128)} %param.16) | copy-start | bytes 61444
  33.0 484.3 %copy-start.4 = (f32[5,128]{1,0:T(8,128)S(1)}, f32[5,128]{1,0:T(8,128)}, u32[]{:S(2)}) copy-start(f32[5,128]{1,0:T(8,128)} %param.17) | copy-start | bytes 7684
  517.4 8.2 %copy-start.5 = (f32[16]{0:T(128)S(1)}, f32[16]{0:T(128)}, u32[]{:S(2)}) copy-start(f32[16]{0:T(128)} %param.18) | copy-start | bytes 196
  525.4 22.3 %copy-start.3 = (f32[1024]{0:T(1024)S(1)}, f32[1024]{0:T(1024)}, u32[]{:S(2)}) copy-start(f32[1024]{0:T(1024)} %param.21) | copy-start | bytes 12292
  526.1 5.8 collective-permute-start
  533.3 95.8 %copy-start = (bf16[128,1152]{0,1:T(8,128)(2,1)}, bf16[128,1152]{0,1:T(8,128)(2,1)S(1)}, u32[]{:S(2)}) copy-start(bf16[128,1152]{0,1:T(8,128)(2,1)S(1)} %multiply_convert_fusion.2) | copy-start | bytes 884740
  629.1 2.2 slice-start
  629.1 6.1 copy-start.7
  631.3 3.9 slice-start.1
Sparse Core Ops, SparseCore 0:
  547.9 80.1 all-gather.1
